TPU v7x, 512 devices: a whole 4x4x16 slice. The times are simulated.
512 devices in a mesh: dp: 64 (over z, x_hi, core), fsdp: 8 (over x_lo, y).
Axes of the slice: x: 4 (x_hi: 2, x_lo: 2; x = x_hi * 2 + x_lo), y: 4, z: 16, core: 2. Of those that a mesh axis runs over, the one named last changes fastest.
Arguments:
- states: bfloat16 [128, 512, 5120], P('dp', None, 'fsdp'), may hold values from -240 to 240
- valid_counts: int32 [128], P('dp'), may hold values from 32 to 512
- section_ids: int32 [128], replicated, may hold values from 0 to 63, never falling along the last dimension, each value on 1 to 6 neighbouring positions
- norm_gain: bfloat16 [5120], P('fsdp'), may hold values from 0.099609375 to 1.8984375
- head_weight: bfloat16 [5120, 2048], P('fsdp'), may hold values from -0.078125 to 0.078125
Outputs:
- embeddings: float32 [64, 3840], P('dp')
Inputs may be any that keep to these rules, and one draw needn't show every extreme that they name: `section_ids`: section numbers never fall along the spans; every one of the 64 sections has 1 to 6 spans.
All inputs are finite; a program needn't handle non-finite values.
Results may differ from a plain program's by a relative error of at most 0.0003.
Values sent between devices are 32-bit elements; how exact they have to be, the bound alone decides.
No kernel may reach another device: no remote copies, remote signals or barrier semaphores. Data moves between devices by JAX's collectives and lax.ppermute only.
A program may use at most 64 MiB of HBM per device.

v0:
```python
import jax
import jax.numpy as jnp
from jax import lax
from jax.sharding import PartitionSpec as P

D = 5120
epsilon = 1e-06


def nested(projected):
    width = projected.shape[1]
    pieces = []
    for level in (width // 8, width // 4, width // 2, width):
        front = projected[:, :level]
        pieces.append(front * lax.rsqrt(jnp.mean(front * front, axis=1, keepdims=True) + epsilon))
    return jnp.concatenate(pieces, axis=1)


def local(states, valid_counts, section_ids, norm_gain, head_weight):
    values = states.astype(jnp.float32)
    partial_squares = jnp.sum(values * values, axis=-1)
    squares = lax.psum(partial_squares, "fsdp")
    scale = lax.rsqrt(squares / D + epsilon)
    slots = jnp.arange(states.shape[1], dtype=jnp.int32)
    used = (slots[None, :] < valid_counts[:, None]).astype(jnp.float32)
    weights = scale * used
    sums = jnp.einsum("cl,cld->cd", weights, values, precision=lax.Precision.HIGHEST)
    pooled = (
        sums / valid_counts.astype(jnp.float32)[:, None] * norm_gain.astype(jnp.float32)[None, :]
    )
    groups = lax.axis_size("dp")
    local_spans = pooled.shape[0]
    sec_local = local_spans // 2
    total_sections = sec_local * groups
    labels = jnp.arange(total_sections, dtype=jnp.int32)
    columns = lax.all_to_all(pooled, "dp", split_axis=1, concat_axis=0, tiled=True)
    member = (section_ids[None, :] == labels[:, None]).astype(jnp.float32)
    section_sums = jnp.dot(member, columns, precision=lax.Precision.HIGHEST)
    width = columns.shape[1]
    weight_part = lax.dynamic_slice_in_dim(head_weight, lax.axis_index("dp") * width, width, 0)
    weight_rows = weight_part.astype(jnp.float32)
    terms = jnp.dot(section_sums, weight_rows, precision=lax.Precision.HIGHEST)
    summed = lax.psum(terms, ("dp", "fsdp"))
    start = lax.axis_index("dp") * sec_local
    projected = lax.dynamic_slice_in_dim(summed, start, sec_local, 0)
    return nested(projected)


def solution(mesh):
    in_specs = (P("dp", None, "fsdp"), P("dp"), P(), P("fsdp"), P("fsdp", None))
    out_specs = P("dp", None)
    return jax.shard_map(local, mesh=mesh, in_specs=in_specs, out_specs=out_specs, check_vma=False)
```

profile of v0, /device:TPU:4, one launch (start us, length us, event | category | flops | bytes accessed | tf_op | source)
XLA Modules:
  0.0 534.0 jit_solution(12853491107874853173)
XLA Ops:
  6.5 0.0 copy-start
  6.5 0.0 copy-start.1
  6.5 0.8 convert_element_type.13
  7.4 0.7 convert_element_type.14
  8.0 1.6 multiply_reduce_fusion
  9.7 19.6 %psum.14 = f32[2,512]{1,0:T(2,128)S(1)} all-reduce(f32[2,512]{1,0:T(2,128)S(1)} %multiply_reduce_fusion), channel_id=1, replica_groups=mesh['dp'=64,'fsdp'=8] {'fsdp'}, use_global_device_ids=true, to_apply=%region_1.0 | all-reduce | flops 1024 | bytes 8192 | tf_op jit(solution)/shard_map/psum | solution.py:22
  29.3 0.7 fusion.5
  30.0 1.9 fusion.6
  31.9 0.1 fusion.4
  32.0 0.1 all_to_all.14
  32.2 0.7 copy.7
  32.8 18.6 %all-to-all-start = ((f32[2,64,10]{2,0,1:T(2,128)}), f32[2,64,10]{2,0,1:T(2,128)S(1)}, u32[]{:S(2)}, u32[]{:S(2)}) async-start(f32[2,64,10]{2,0,1:T(2,128)} %copy.7), calls=%async_computation | async-start | bytes 131072 | tf_op jit(solution)/shard_map/all_to_all | solution.py:36
  51.5 0.0 all-reduce.2.cloned.1.call-start
  51.5 13.8 %all-to-all-done = f32[2,64,10]{2,0,1:T(2,128)S(1)} async-done(((f32[2,64,10]{2,0,1:T(2,128)}), f32[2,64,10]{2,0,1:T(2,128)S(1)}, u32[]{:S(2)}, u32[]{:S(2)}) %all-to-all-start) | async-done | bytes 5152 | tf_op jit(solution)/shard_map/all_to_all | solution.py:36
  65.3 0.0 copy-done.1
  65.3 0.2 fusion.2
  65.5 0.0 copy-done
  65.5 1.3 fusion
  66.8 0.0 all-reduce.2.cloned.1.call-update
  66.8 448.4 %all-reduce.2.cloned.1.call-done = f32[64,2048]{1,0:T(8,128)} async-done(((f32[64,2048]{1,0:T(8,128)}), f32[64,2048]{1,0:T(8,128)}) %all-reduce.2.cloned.1.call-update) | async-done | bytes 524304 | tf_op jit(solution)/shard_map/psum | solution.py:43
  515.2 1.5 multiply_reduce_fusion.1
  517.3 1.4 multiply_reduce_fusion.2
  519.4 1.3 multiply_reduce_fusion.3
  521.4 1.3 multiply_reduce_fusion.4
  523.4 0.7 broadcast_multiply_fusion.3
  524.1 0.7 broadcast_multiply_fusion.2
  524.9 0.8 broadcast_multiply_fusion.1
  525.6 0.9 broadcast_multiply_fusion
  526.5 0.6 pad_maximum_fusion
Async XLA Ops:
  6.5 59.0 %copy-start = (bf16[640,2048]{1,0:T(8,128)(2,1)S(1)}, bf16[640,2048]{1,0:T(8,128)(2,1)}, u32[]{:S(2)}) copy-start(bf16[640,2048]{1,0:T(8,128)(2,1)} %param.9) | copy-start | bytes 7864324
  6.5 58.8 %copy-start.1 = (s32[128]{0:T(128)S(1)}, s32[128]{0:T(128)}, u32[]{:S(2)}) copy-start(s32[128]{0:T(128)} %param.7) | copy-start | bytes 1540
  32.8 32.5 %all-to-all-start = ((f32[2,64,10]{2,0,1:T(2,128)}), f32[2,64,10]{2,0,1:T(2,128)S(1)}, u32[]{:S(2)}, u32[]{:S(2)}) async-start(f32[2,64,10]{2,0,1:T(2,128)} %copy.7), calls=%async_computation | async-start | bytes 131072 | tf_op jit(solution)/shard_map/all_to_all | solution.py:36
  51.5 463.7 %all-reduce.2.cloned.1.call-start = ((), (), s32[]{:S(2)}) async-start(), calls=%async_computation.1 | async-start | bytes 1048576 | tf_op jit(solution)/shard_map/psum | solution.py:43
Sparse Core Ops, SparseCore 0:
  66.9 448.2 all-reduce.1
where the time goes:
time: 535 us; the launch traced here: 534 us
  waiting for transfers between devices  462 us (86%)
  blocking collectives  19.6 us (4%)
  starting transfers between devices  18.7 us (3%)
  between operations  16.2 us (3%)
  other arithmetic  13.1 us (2%)
    psum x1, waiting for transfers between devices, local(): summed = lax.psum(terms, ('dp', 'fsdp'))  448 us
    psum x1, blocking collectives, local(): squares = lax.psum(partial_squares, 'fsdp')  19.6 us
    all_to_all x1, starting transfers between devices, local(): lax.all_to_all(pooled, 'dp', split_axis=1, concat_axis=0, tiled=True)  18.6 us
    all_to_all x1, waiting for transfers between devices, local(): lax.all_to_all(pooled, 'dp', split_axis=1, concat_axis=0, tiled=True)  13.8 us
  transfers between devices with their start and end apart: 2, of which 2 were waited for; matrix products, arithmetic and copies ran while one was open for 0% of the time, Pallas kernels for 0%

commit v1 on v0

--- a/solution.py
+++ b/solution.py
@@ -40,7 +40,7 @@
     weight_part = lax.dynamic_slice_in_dim(head_weight, lax.axis_index("dp") * width, width, 0)
     weight_rows = weight_part.astype(jnp.float32)
     terms = jnp.dot(section_sums, weight_rows, precision=lax.Precision.HIGHEST)
-    summed = lax.psum(terms, ("dp", "fsdp"))
+    summed = lax.psum(lax.psum(terms, "dp"), "fsdp")
     start = lax.axis_index("dp") * sec_local
     projected = lax.dynamic_slice_in_dim(summed, start, sec_local, 0)
     return nested(projected)

time: 535 us -> 691 us (1.29)
  waiting for transfers between devices: 462 us -> 619 us
    psum x1 -> x2, waiting for transfers between devices: 448 us -> 605 us  [local(): summed = lax.psum(lax.psum(terms, 'dp'), 'fsdp')]
  transfers between devices with their start and end apart: 2 -> 3, of which waited for: 2 -> 3; matrix products, arithmetic and copies ran while one was open for 0% -> 0% of each run, Pallas kernels for 0% -> 0%
where the time goes in v1:
time: 691 us; the launch traced here: 690 us
  waiting for transfers between devices  619 us (90%)
  blocking collectives  19.6 us (3%)
  starting transfers between devices  18.7 us (3%)
  between operations  16.2 us (2%)
  other arithmetic  13.1 us (2%)
    psum x2, waiting for transfers between devices, local(): summed = lax.psum(lax.psum(terms, 'dp'), 'fsdp')  605 us
    psum x1, blocking collectives, local(): squares = lax.psum(partial_squares, 'fsdp')  19.6 us
    all_to_all x1, starting transfers between devices, local(): lax.all_to_all(pooled, 'dp', split_axis=1, concat_axis=0, tiled=True)  18.6 us
  transfers between devices with their start and end apart: 3, of which 3 were waited for; matrix products, arithmetic and copies ran while one was open for 0% of the time, Pallas kernels for 0%

profile of v1, /device:TPU:4, one launch (start us, length us, event | category | flops | bytes accessed | tf_op | source)
XLA Modules:
  0.0 690.5 jit_solution(8173464733046810673)
XLA Ops:
  6.5 0.0 copy-start
  6.5 0.0 copy-start.1
  6.5 0.8 convert_element_type.13
  7.4 0.7 convert_element_type.14
  8.0 1.6 multiply_reduce_fusion
  9.7 19.6 %psum.21 = f32[2,512]{1,0:T(2,128)S(1)} all-reduce(f32[2,512]{1,0:T(2,128)S(1)} %multiply_reduce_fusion), channel_id=1, replica_groups=mesh['dp'=64,'fsdp'=8] {'fsdp'}, use_global_device_ids=true, to_apply=%region_1.0 | all-reduce | flops 1024 | bytes 8192 | tf_op jit(solution)/shard_map/psum | solution.py:22
  29.3 0.7 fusion.5
  30.0 1.9 fusion.6
  31.9 0.1 fusion.4
  32.0 0.1 all_to_all.14
  32.2 0.7 copy.7
  32.8 18.6 %all-to-all-start = ((f32[2,64,10]{2,0,1:T(2,128)}), f32[2,64,10]{2,0,1:T(2,128)S(1)}, u32[]{:S(2)}, u32[]{:S(2)}) async-start(f32[2,64,10]{2,0,1:T(2,128)} %copy.7), calls=%async_computation | async-start | bytes 131072 | tf_op jit(solution)/shard_map/all_to_all | solution.py:36
  51.5 0.0 all-reduce.3.cloned.1.call-start
  51.5 13.8 %all-to-all-done = f32[2,64,10]{2,0,1:T(2,128)S(1)} async-done(((f32[2,64,10]{2,0,1:T(2,128)}), f32[2,64,10]{2,0,1:T(2,128)S(1)}, u32[]{:S(2)}, u32[]{:S(2)}) %all-to-all-start) | async-done | bytes 5152 | tf_op jit(solution)/shard_map/all_to_all | solution.py:36
  65.3 0.0 copy-done.1
  65.3 0.2 fusion.2
  65.5 0.0 copy-done
  65.5 1.3 fusion
  66.8 0.0 all-reduce.3.cloned.1.call-update
  66.8 0.0 all-reduce.5.cloned.1.call-start
  66.8 512.3 %all-reduce.3.cloned.1.call-done = f32[64,2048]{1,0:T(8,128)} async-done(((f32[64,2048]{1,0:T(8,128)}), f32[64,2048]{1,0:T(8,128)}) %all-reduce.3.cloned.1.call-update) | async-done | bytes 524304 | tf_op jit(solution)/shard_map/psum | solution.py:43
  579.1 0.0 all-reduce.5.cloned.1.call-update
  579.2 92.5 %all-reduce.5.cloned.1.call-done = f32[64,2048]{1,0:T(8,128)} async-done(((f32[64,2048]{1,0:T(8,128)}), f32[64,2048]{1,0:T(8,128)}) %all-reduce.5.cloned.1.call-update) | async-done | bytes 524304 | tf_op jit(solution)/shard_map/psum | solution.py:43
  671.7 1.5 multiply_reduce_fusion.1
  673.9 1.4 multiply_reduce_fusion.2
  675.9 1.3 multiply_reduce_fusion.3
  678.0 1.3 multiply_reduce_fusion.4
  680.0 0.7 broadcast_multiply_fusion.3
  680.7 0.7 broadcast_multiply_fusion.2
  681.4 0.8 broadcast_multiply_fusion.1
  682.2 0.9 broadcast_multiply_fusion
  683.0 0.6 pad_maximum_fusion
Async XLA Ops:
  6.5 59.0 %copy-start = (bf16[640,2048]{1,0:T(8,128)(2,1)S(1)}, bf16[640,2048]{1,0:T(8,128)(2,1)}, u32[]{:S(2)}) copy-start(bf16[640,2048]{1,0:T(8,128)(2,1)} %param.9) | copy-start | bytes 7864324
  6.5 58.8 %copy-start.1 = (s32[128]{0:T(128)S(1)}, s32[128]{0:T(128)}, u32[]{:S(2)}) copy-start(s32[128]{0:T(128)} %param.7) | copy-start | bytes 1540
  32.8 32.5 %all-to-all-start = ((f32[2,64,10]{2,0,1:T(2,128)}), f32[2,64,10]{2,0,1:T(2,128)S(1)}, u32[]{:S(2)}, u32[]{:S(2)}) async-start(f32[2,64,10]{2,0,1:T(2,128)} %copy.7), calls=%async_computation | async-start | bytes 131072 | tf_op jit(solution)/shard_map/all_to_all | solution.py:36
  51.5 527.7 %all-reduce.3.cloned.1.call-start = ((), (), s32[]{:S(2)}) async-start(), calls=%async_computation.1 | async-start | bytes 1048576 | tf_op jit(solution)/shard_map/psum | solution.py:43
  66.8 604.9 %all-reduce.5.cloned.1.call-start = ((), (), s32[]{:S(2)}) async-start(), calls=%async_computation.2 | async-start | bytes 1048576 | tf_op jit(solution)/shard_map/psum | solution.py:43
Sparse Core Ops, SparseCore 0:
  66.9 512.1 all-reduce.2
  582.3 89.3 all-reduce.4
